TPU v7x, 256 devices: a whole 4x4x8 slice. The times are simulated.
256 devices in a mesh: dp: 32 (over x_lo, z, core), blk: 8 (over y, x_hi).
Axes of the slice: x: 4 (x_hi: 2, x_lo: 2; x = x_hi * 2 + x_lo), y: 4, z: 8, core: 2. Of those that a mesh axis runs over, the one named last changes fastest.
Arguments:
- inputs: bfloat16 [8, 16384, 4096], P('blk', 'dp'), may hold values from -6 to 6
- out_grads: bfloat16 [8, 16384, 4096], P('blk', 'dp'), may hold values from -8 to 8
- test_matrix: bfloat16 [8, 4096, 256], P('blk'), may hold values from -6 to 6
- momentum: bfloat16 [8, 4096, 4096], P(None, 'blk', 'dp'), may hold values from -6 to 6
Outputs:
- update: bfloat16 [8, 4096, 4096], P(None, 'blk', 'dp')
All inputs are finite; a program needn't handle non-finite values.
Results may differ from a plain program's by a relative error of at most 0.0035.
Values may be sent and summed in bfloat16 or wider, within the bound.
No kernel may reach another device: no remote copies, remote signals or barrier semaphores. Data moves between devices by JAX's collectives and lax.ppermute only.
A program may use at most 128 MiB of HBM per device.

v0:
```python
import jax
import jax.numpy as jnp
from jax import lax
from jax.sharding import PartitionSpec as P


def inner_gram(columns):
    return lax.dot_general(
        columns, columns, (((0,), (0,)), ((), ())), precision=lax.Precision.HIGHEST
    )


def cholesky_pass(columns, gram_matrix):
    lower_factor = jnp.linalg.cholesky(gram_matrix)
    return lax.linalg.triangular_solve(
        lower_factor, columns, left_side=False, lower=True, transpose_a=True
    )


def shards(inputs, out_grads, test_matrix, momentum):
    features = inputs[0]
    errors = out_grads[0]
    probes = test_matrix[0]
    replicas = lax.axis_size("dp")
    scale = 1.0 / (features.shape[1] * features.shape[0] * replicas)
    columns = lax.all_to_all(momentum, "blk", split_axis=0, concat_axis=1, tiled=True)[0]
    projected = jnp.dot(features, probes, preferred_element_type=jnp.float32).astype(jnp.bfloat16)
    token_gram = lax.dot_general(
        errors, errors, (((1,), (1,)), ((), ())), preferred_element_type=jnp.float32
    ).astype(jnp.bfloat16)
    mixed_rows = jnp.dot(token_gram, projected, preferred_element_type=jnp.float32).astype(
        jnp.bfloat16
    )
    sketch_term = (
        lax.dot_general(
            features, mixed_rows, (((0,), (0,)), ((), ())), preferred_element_type=jnp.float32
        )
        * scale
    )
    sketch = lax.psum(sketch_term, "dp")
    basis = cholesky_pass(sketch, inner_gram(sketch)).astype(jnp.bfloat16)
    reduced = jnp.dot(features, basis, preferred_element_type=jnp.float32).astype(jnp.bfloat16)
    shaped = jnp.dot(token_gram, reduced, preferred_element_type=jnp.float32).astype(jnp.bfloat16)
    core_term = (
        lax.dot_general(
            reduced, shaped, (((0,), (0,)), ((), ())), preferred_element_type=jnp.float32
        )
        * scale
    )
    core_matrix = lax.psum(core_term, "dp")
    shifted = core_matrix + jnp.eye(core_matrix.shape[0], dtype=jnp.float32)
    lower_factor = jnp.linalg.cholesky(shifted)
    half_solved = lax.linalg.triangular_solve(lower_factor, core_matrix, left_side=True, lower=True)
    factor = lax.linalg.triangular_solve(
        lower_factor, half_solved, left_side=True, lower=True, transpose_a=True
    )
    coeffs = lax.dot_general(
        basis, columns, (((0,), (0,)), ((), ())), preferred_element_type=jnp.float32
    )
    scaled = jnp.dot(factor, coeffs, precision=lax.Precision.HIGHEST).astype(jnp.bfloat16)
    fresh = (
        columns.astype(jnp.float32) - jnp.dot(basis, scaled, preferred_element_type=jnp.float32)
    ).astype(jnp.bfloat16)
    return lax.all_to_all(fresh[None], "blk", split_axis=1, concat_axis=0, tiled=True)


def solution(mesh):
    in_specs = (
        P("blk", "dp", None),
        P("blk", "dp", None),
        P("blk", None, None),
        P(None, "blk", "dp"),
    )
    out_specs = P(None, "blk", "dp")
    return jax.shard_map(shards, mesh=mesh, in_specs=in_specs, out_specs=out_specs, check_vma=False)
```

profile of v0, /device:TPU:1, one launch (start us, length us, event | category | flops | bytes accessed | tf_op | source)
XLA Modules:
  0.0 706.3 jit_solution(12601974615667945552)
XLA Ops:
  6.5 6.0 fusion.13
  13.8 5.9 fusion
  19.7 7.5 %all-to-all-start = ((bf16[8,512,128]{2,1,0:T(8,128)(2,1)}), bf16[8,512,128]{2,1,0:T(8,128)(2,1)}, u32[]{:S(2)}, u32[]{:S(2)}) async-start(bf16[8,512,128]{2,1,0:T(8,128)(2,1)} %param.8), calls=%async_computation | async-start | bytes 2097152 | tf_op jit(solution)/shard_map/all_to_all | solution.py:26
  27.3 231.4 %all-reduce.4.cloned.1.call-done = f32[4096,256]{0,1:T(8,128)} async-done(((f32[4096,256]{0,1:T(8,128)}), f32[4096,256]{0,1:T(8,128)}) %all-reduce.4.cloned.1.call-update) | async-done | bytes 4194320 | tf_op jit(solution)/shard_map/psum | solution.py:40
  258.7 12.1 %fusion.53 = f32[256,256]{1,0:T(8,128)S(1)} fusion(f32[4096,256]{0,1:T(8,128)} %all-reduce.4.cloned.1.call-done), kind=kOutput, calls=%fused_computation.90 | convolution fusion | flops 3221225472 | bytes 4456448 | tf_op jit(solution)/shard_map/dot_general | solution.py:8
  271.0 11.7 %cholesky.130 = f32[128,128]{1,0:T(8,128)S(1)} custom-call(f32[128,128]{1,0:T(8,128)S(1)} %cholesky.194), custom_call_target="Cholesky" | custom-call | tf_op jit(solution)/shard_map/jit(cholesky)/cholesky | solution.py:14
  282.8 9.8 %custom-call.19 = f32[1,128,128]{1,2,0:T(8,128)S(1)} custom-call(f32[1,128,128]{2,1,0:T(8,128)S(1)} %get-tuple-element.49), custom_call_target="InvertDiagBlocksLowerTriangular" | custom-call | tf_op jit(solution)/shard_map/jit(cholesky)/cholesky | solution.py:14
  293.1 11.7 %cholesky.147 = f32[128,128]{1,0:T(8,128)S(1)} custom-call(f32[128,128]{1,0:T(8,128)S(1)} %convolution_subtract_fusion.5), custom_call_target="Cholesky" | custom-call | tf_op jit(solution)/shard_map/jit(cholesky)/cholesky | solution.py:14
  306.9 3.9 while.2
  307.5 1.3 bitcast_dynamic-update-slice_fusion.4
  309.4 1.3 bitcast_dynamic-update-slice_fusion.4
  310.8 19.9 %custom-call.16 = f32[2,128,128]{1,2,0:T(8,128)S(1)} custom-call(f32[2,128,128]{2,1,0:T(8,128)S(1)} %get-tuple-element.13), custom_call_target="InvertDiagBlocksLowerTriangular" | custom-call | tf_op jit(solution)/shard_map/triangular_solve | solution.py:15
  330.7 3.7 fusion.52
  334.4 2.0 convolution_subtract_fusion.1
  336.5 2.0 convolution_convert_fusion
  339.4 1.3 fusion.21
  340.7 1.3 fusion.25
  342.1 2.6 fusion.26
  344.7 216.2 %all-reduce.6.cloned.1.call-done = f32[256,256]{0,1:T(8,128)} async-done(((f32[256,256]{0,1:T(8,128)}), f32[256,256]{0,1:T(8,128)}) %all-reduce.6.cloned.1.call-update) | async-done | bytes 262160 | tf_op jit(solution)/shard_map/psum | solution.py:50
  563.1 12.1 %cholesky.164 = f32[128,128]{1,0:T(8,128)S(1)} custom-call(f32[128,128]{1,0:T(8,128)S(1)} %cholesky.197), custom_call_target="Cholesky" | custom-call | tf_op jit(solution)/shard_map/jit(cholesky)/cholesky | solution.py:52
  575.3 9.8 %custom-call.20 = f32[1,128,128]{1,2,0:T(8,128)S(1)} custom-call(f32[1,128,128]{2,1,0:T(8,128)S(1)} %get-tuple-element.45), custom_call_target="InvertDiagBlocksLowerTriangular" | custom-call | tf_op jit(solution)/shard_map/jit(cholesky)/cholesky | solution.py:52
  585.5 11.7 %cholesky.181 = f32[128,128]{1,0:T(8,128)S(1)} custom-call(f32[128,128]{1,0:T(8,128)S(1)} %convolution_subtract_fusion.4), custom_call_target="Cholesky" | custom-call | tf_op jit(solution)/shard_map/jit(cholesky)/cholesky | solution.py:52
  599.9 3.8 while.3
  600.5 1.3 bitcast_dynamic-update-slice_fusion.5
  602.4 1.3 bitcast_dynamic-update-slice_fusion.5
  603.7 19.7 %custom-call.17 = f32[2,128,128]{1,2,0:T(8,128)S(1)} custom-call(f32[2,128,128]{2,1,0:T(8,128)S(1)} %get-tuple-element.21), custom_call_target="InvertDiagBlocksLowerTriangular" | custom-call | tf_op jit(solution)/shard_map/triangular_solve | solution.py:54
  625.7 2.7 fusion.2
  628.4 17.2 %copy.23 = bf16[1,4096,128]{2,0,1:T(2,128)(2,1)} copy(bf16[1,4096,128]{2,1,0:T(8,128)(2,1)S(1)} %fusion.2) | data formatting | bytes 2097152 | tf_op jit(solution)/shard_map/broadcast_in_dim | solution.py:64
  646.1 23.4 %reduce.8 = bf16[4096,128]{1,0:T(8,128)(2,1)S(1)} reduce(bf16[4096,1,128]{2,1,0:T(2,128)(2,1)} %bitcast.111, bf16[]{:T(256)} %broadcast.127), dimensions={1}, to_apply=%bitcast.97.reduce_sub_computation | reduce | bytes 2097154
  670.6 22.5 %all_to_all.21 = bf16[8,2,32768]{2,1,0:T(2,128)(2,1)S(1)} all-to-all(bf16[8,2,32768]{2,1,0:T(2,128)(2,1)} %reshape.68), channel_id=1, replica_groups=mesh['dp'=32,'blk'=8] {'blk'}, dimensions={0} | all-to-all | bytes 2097152 | tf_op jit(solution)/shard_map/all_to_all | solution.py:64
  693.1 3.5 reshape.69
  696.6 2.7 copy.21
  (63 shorter events, 14.1 us)
Async XLA Ops:
  6.5 6.0 copy-start
  6.5 252.2 %all-reduce.4.cloned.1.call-start = ((), (), s32[]{:S(2)}) async-start(), calls=%async_computation.2 | async-start | bytes 8388608 | tf_op jit(solution)/shard_map/psum | solution.py:40
  6.5 6.0 copy-start.2
  19.7 322.3 %all-to-all-start = ((bf16[8,512,128]{2,1,0:T(8,128)(2,1)}), bf16[8,512,128]{2,1,0:T(8,128)(2,1)}, u32[]{:S(2)}, u32[]{:S(2)}) async-start(bf16[8,512,128]{2,1,0:T(8,128)(2,1)} %param.8), calls=%async_computation | async-start | bytes 2097152 | tf_op jit(solution)/shard_map/all_to_all | solution.py:26
  27.3 533.6 %all-reduce.6.cloned.1.call-start = ((), (), s32[]{:S(2)}) async-start(), calls=%async_computation.3 | async-start | bytes 524288 | tf_op jit(solution)/shard_map/psum | solution.py:50
  330.6 3.8 copy-start.1
  334.4 4.1 copy-start.6
  334.4 5.0 copy-start.3
  338.5 1.0 copy-start.5
  560.9 62.5 %copy-start.4 = (f32[256,256]{0,1:T(8,128)S(1)}, f32[256,256]{0,1:T(8,128)}, u32[]{:S(2)}) copy-start(f32[256,256]{0,1:T(8,128)} %all-reduce.6.cloned.1.call-done) | copy-start | bytes 786436
Sparse Core Ops, SparseCore 0:
  19.9 238.8 all-reduce.3
  342.2 218.6 all-reduce.5
where the time goes:
time: 713 us; the launch traced here: 706 us
  waiting for transfers between devices  448 us (63%)
  other arithmetic  134 us (19%)
  matrix products  44 us (6%)
  local copies, waits for them, and re-layouts  34 us (5%)
  blocking collectives  22.5 us (3%)
  between operations  16.4 us (2%)
  starting transfers between devices  7.55 us (1%)
    psum x1, waiting for transfers between devices, shards(): sketch = lax.psum(sketch_term, 'dp')  231 us
    psum x1, waiting for transfers between devices, shards(): core_matrix = lax.psum(core_term, 'dp')  216 us
    another operation x7, other arithmetic, shards(): lower_factor = jnp.linalg.cholesky(shifted)  35 us
    another operation x6, other arithmetic, cholesky_pass(): lower_factor = jnp.linalg.cholesky(gram_matrix)  34 us
    unnamed x1, other arithmetic  23.4 us
    all_to_all x1, blocking collectives, shards(): lax.all_to_all(fresh[None], 'blk', split_axis=1, concat_axis=0, tiled=True)  22.5 us
    another operation x3, other arithmetic, cholesky_pass(): lax.linalg.triangular_solve(lower_factor, columns, left_side=False, lower...  19.9 us
    another operation x2, other arithmetic, shards(): lax.linalg.triangular_solve(lower_factor, half_solved, left_side=True, lo...  19.7 us
  transfers between devices with their start and end apart: 3, of which 2 were waited for; matrix products, arithmetic and copies ran while one was open for 12% of the time, Pallas kernels for 0%

commit v1 on v0

--- a/solution.py
+++ b/solution.py
@@ -61,7 +61,12 @@
     fresh = (
         columns.astype(jnp.float32) - jnp.dot(basis, scaled, preferred_element_type=jnp.float32)
     ).astype(jnp.bfloat16)
-    return lax.all_to_all(fresh[None], "blk", split_axis=1, concat_axis=0, tiled=True)
+    return jnp.concatenate(
+        lax.all_to_all(
+            jnp.stack(jnp.split(fresh[None], lax.axis_size("blk"), axis=1)), "blk", 0, 0
+        ),
+        axis=0,
+    )
 
 
 def solution(mesh):

time: 713 us -> 665 us (0.933)
  other arithmetic: 134 us -> 110 us
  local copies, waits for them, and re-layouts: 34 us -> 10.1 us
    unnamed x1 -> x0, other arithmetic: 23.4 us -> none
    broadcast_in_dim x1 -> x0, local copies, waits for them, and re-layouts: 17.2 us -> none  [shards(): fresh[None]]
  transfers between devices with their start and end apart: 3 -> 3, of which waited for: 2 -> 2; matrix products, arithmetic and copies ran while one was open for 12% -> 13% of each run, Pallas kernels for 0% -> 0%
where the time goes in v1:
time: 665 us; the launch traced here: 659 us
  waiting for transfers between devices  448 us (67%)
  other arithmetic  110 us (17%)
  matrix products  44.2 us (7%)
  blocking collectives  22.3 us (3%)
  between operations  16.5 us (2%)
  local copies, waits for them, and re-layouts  10.1 us (2%)
  starting transfers between devices  7.56 us (1%)
    psum x1, waiting for transfers between devices, shards(): sketch = lax.psum(sketch_term, 'dp')  231 us
    psum x1, waiting for transfers between devices, shards(): core_matrix = lax.psum(core_term, 'dp')  216 us
    another operation x7, other arithmetic, shards(): lower_factor = jnp.linalg.cholesky(shifted)  34.8 us
    another operation x6, other arithmetic, cholesky_pass(): lower_factor = jnp.linalg.cholesky(gram_matrix)  34 us
    all_to_all x1, blocking collectives, shards(): lax.all_to_all(jnp.stack(jnp.split(fresh[None], lax.axis_size('blk'), axi...  22.3 us
    another operation x3, other arithmetic, cholesky_pass(): lax.linalg.triangular_solve(lower_factor, columns, left_side=False, lower...  19.9 us
    another operation x2, other arithmetic, shards(): lax.linalg.triangular_solve(lower_factor, half_solved, left_side=True, lo...  19.7 us
  transfers between devices with their start and end apart: 3, of which 2 were waited for; matrix products, arithmetic and copies ran while one was open for 13% of the time, Pallas kernels for 0%

profile of v1, /device:TPU:1, one launch (start us, length us, event | category | flops | bytes accessed | tf_op | source)
XLA Modules:
  0.0 658.9 jit_solution(8992191758235351324)
XLA Ops:
  6.5 6.0 fusion.13
  12.5 1.3 fusion.16
  13.8 5.9 fusion
  19.7 7.5 %all-to-all-start = ((bf16[8,512,128]{2,1,0:T(8,128)(2,1)}), bf16[8,512,128]{2,1,0:T(8,128)(2,1)}, u32[]{:S(2)}, u32[]{:S(2)}) async-start(bf16[8,512,128]{2,1,0:T(8,128)(2,1)} %param.8), calls=%async_computation | async-start | bytes 2097152 | tf_op jit(solution)/shard_map/all_to_all | solution.py:26
  27.3 231.4 %all-reduce.4.cloned.1.call-done = f32[4096,256]{0,1:T(8,128)} async-done(((f32[4096,256]{0,1:T(8,128)}), f32[4096,256]{0,1:T(8,128)}) %all-reduce.4.cloned.1.call-update) | async-done | bytes 4194320 | tf_op jit(solution)/shard_map/psum | solution.py:40
  258.7 12.4 %fusion.61 = f32[256,256]{1,0:T(8,128)S(1)} fusion(f32[4096,256]{0,1:T(8,128)} %all-reduce.4.cloned.1.call-done), kind=kOutput, calls=%fused_computation.105 | convolution fusion | flops 3221225472 | bytes 4456448 | tf_op jit(solution)/shard_map/dot_general | solution.py:8
  271.3 11.7 %cholesky.130 = f32[128,128]{1,0:T(8,128)S(1)} custom-call(f32[128,128]{1,0:T(8,128)S(1)} %cholesky.194), custom_call_target="Cholesky" | custom-call | tf_op jit(solution)/shard_map/jit(cholesky)/cholesky | solution.py:14
  283.1 9.8 %custom-call.19 = f32[1,128,128]{1,2,0:T(8,128)S(1)} custom-call(f32[1,128,128]{2,1,0:T(8,128)S(1)} %get-tuple-element.49), custom_call_target="InvertDiagBlocksLowerTriangular" | custom-call | tf_op jit(solution)/shard_map/jit(cholesky)/cholesky | solution.py:14
  293.4 11.7 %cholesky.147 = f32[128,128]{1,0:T(8,128)S(1)} custom-call(f32[128,128]{1,0:T(8,128)S(1)} %convolution_subtract_fusion.5), custom_call_target="Cholesky" | custom-call | tf_op jit(solution)/shard_map/jit(cholesky)/cholesky | solution.py:14
  307.2 3.9 while.2
  307.8 1.3 bitcast_dynamic-update-slice_fusion.4
  309.7 1.3 bitcast_dynamic-update-slice_fusion.4
  311.1 19.8 %custom-call.16 = f32[2,128,128]{1,2,0:T(8,128)S(1)} custom-call(f32[2,128,128]{2,1,0:T(8,128)S(1)} %get-tuple-element.13), custom_call_target="InvertDiagBlocksLowerTriangular" | custom-call | tf_op jit(solution)/shard_map/triangular_solve | solution.py:15
  330.9 3.7 fusion.60
  334.7 2.0 convolution_subtract_fusion.1
  336.7 2.0 convolution_convert_fusion
  339.7 1.3 fusion.21
  341.0 1.3 fusion.25
  342.4 2.5 fusion.26
  344.9 216.3 %all-reduce.6.cloned.1.call-done = f32[256,256]{0,1:T(8,128)} async-done(((f32[256,256]{0,1:T(8,128)}), f32[256,256]{0,1:T(8,128)}) %all-reduce.6.cloned.1.call-update) | async-done | bytes 262160 | tf_op jit(solution)/shard_map/psum | solution.py:50
  561.2 1.0 convert_add_fusion
  562.4 1.0 fusion.30
  563.4 11.9 %cholesky.164 = f32[128,128]{1,0:T(8,128)S(1)} custom-call(f32[128,128]{1,0:T(8,128)S(1)} %cholesky.197), custom_call_target="Cholesky" | custom-call | tf_op jit(solution)/shard_map/jit(cholesky)/cholesky | solution.py:52
  575.3 9.8 %custom-call.20 = f32[1,128,128]{1,2,0:T(8,128)S(1)} custom-call(f32[1,128,128]{2,1,0:T(8,128)S(1)} %get-tuple-element.45), custom_call_target="InvertDiagBlocksLowerTriangular" | custom-call | tf_op jit(solution)/shard_map/jit(cholesky)/cholesky | solution.py:52
  585.6 11.7 %cholesky.181 = f32[128,128]{1,0:T(8,128)S(1)} custom-call(f32[128,128]{1,0:T(8,128)S(1)} %convolution_subtract_fusion.4), custom_call_target="Cholesky" | custom-call | tf_op jit(solution)/shard_map/jit(cholesky)/cholesky | solution.py:52
  600.0 3.8 while.3
  600.6 1.3 bitcast_dynamic-update-slice_fusion.5
  602.5 1.3 bitcast_dynamic-update-slice_fusion.5
  603.8 19.7 %custom-call.17 = f32[2,128,128]{1,2,0:T(8,128)S(1)} custom-call(f32[2,128,128]{2,1,0:T(8,128)S(1)} %get-tuple-element.21), custom_call_target="InvertDiagBlocksLowerTriangular" | custom-call | tf_op jit(solution)/shard_map/triangular_solve | solution.py:54
  625.8 2.6 fusion.2
  628.6 22.3 %all_to_all.14 = bf16[8,1,512,128]{3,2,1,0:T(8,128)(2,1)S(1)} all-to-all(bf16[8,1,512,128]{3,2,1,0:T(8,128)(2,1)S(1)} %fusion.32), channel_id=1, replica_groups=mesh['dp'=32,'blk'=8] {'blk'}, dimensions={0} | all-to-all | bytes 2097152 | tf_op jit(solution)/shard_map/all_to_all | solution.py:65
  650.9 1.0 copy.41
  (66 shorter events, 9.4 us)
Async XLA Ops:
  6.5 6.0 copy-start
  6.5 252.2 %all-reduce.4.cloned.1.call-start = ((), (), s32[]{:S(2)}) async-start(), calls=%async_computation.2 | async-start | bytes 8388608 | tf_op jit(solution)/shard_map/psum | solution.py:40
  6.5 6.0 copy-start.2
  19.7 322.6 %all-to-all-start = ((bf16[8,512,128]{2,1,0:T(8,128)(2,1)}), bf16[8,512,128]{2,1,0:T(8,128)(2,1)}, u32[]{:S(2)}, u32[]{:S(2)}) async-start(bf16[8,512,128]{2,1,0:T(8,128)(2,1)} %param.8), calls=%async_computation | async-start | bytes 2097152 | tf_op jit(solution)/shard_map/all_to_all | solution.py:26
  27.3 533.9 %all-reduce.6.cloned.1.call-start = ((), (), s32[]{:S(2)}) async-start(), calls=%async_computation.3 | async-start | bytes 524288 | tf_op jit(solution)/shard_map/psum | solution.py:50
  330.9 3.8 copy-start.1
  334.7 4.1 copy-start.6
  334.7 5.0 copy-start.3
  338.7 1.0 copy-start.5
  561.2 62.3 %copy-start.4 = (f32[256,256]{0,1:T(8,128)S(1)}, f32[256,256]{0,1:T(8,128)}, u32[]{:S(2)}) copy-start(f32[256,256]{0,1:T(8,128)} %all-reduce.6.cloned.1.call-done) | copy-start | bytes 786436
Sparse Core Ops, SparseCore 0:
  19.9 238.8 all-reduce.3
  342.5 218.6 all-reduce.5
